TPU v7x, 32 devices: a whole 2x2x4 slice. The times are simulated.
32 devices in a mesh: row: 8 (over y, x, core), col: 4 (over z).
Axes of the slice: x: 2, y: 2, z: 4, core: 2. Of those that a mesh axis runs over, the one named last changes fastest.
Arguments:
- pair_rep: bfloat16 [128, 128, 128], P(('row', 'col')), may hold values from -16 to 16
- tile_mask: int32 [1, 1], replicated, may hold values from 0 to 1, as said below
- chain_ids: int32 [128], replicated, may hold values from 0 to 3, never falling along the last dimension, each value on 1 to 64 neighbouring positions
- chain_bias: float32 [2, 4], replicated, may hold values from -6 to 6
- row_project: bfloat16 [128, 512], replicated, may hold values from -0.5 to 0.5
- row_bias_proj: bfloat16 [128, 4], replicated, may hold values from -36 to 36
- row_output: bfloat16 [128, 128], replicated, may hold values from -0.5 to 0.5
- col_project: bfloat16 [128, 512], replicated, may hold values from -0.5 to 0.5
- col_bias_proj: bfloat16 [128, 4], replicated, may hold values from -36 to 36
- col_output: bfloat16 [128, 128], replicated, may hold values from -0.5 to 0.5
- tri_left: bfloat16 [128, 256], replicated, may hold values from -0.5 to 0.5
- tri_right: bfloat16 [128, 256], replicated, may hold values from -0.5 to 0.5
- tri_gate: bfloat16 [128, 128], replicated, may hold values from -0.5 to 0.5
- tri_output: bfloat16 [128, 128], replicated, may hold values from -1.5 to 1.5
Outputs:
- pair_out: bfloat16 [128, 128, 128], P('row', 'col')
Inputs may be any that keep to these rules, and one draw needn't show every extreme that they name: `tile_mask`: every diagonal entry is 1. `chain_ids`: chain numbers never fall along the residues.
All inputs are finite; a program needn't handle non-finite values.
Results may differ from a plain program's by a relative error of at most 0.018.
Values may be sent and summed in bfloat16 or wider, within the bound.
No kernel may reach another device: no remote copies, remote signals or barrier semaphores. Data moves between devices by JAX's collectives and lax.ppermute only.
A program may use at most 64 MiB of HBM per device.

v0:
```python
import jax
import jax.numpy as jnp
from jax import lax
from jax.sharding import PartitionSpec as P


def layer_norm(values):
    values = values.astype(jnp.float32)
    center = values - jnp.mean(values, axis=-1, keepdims=True)
    spread = jnp.mean(center * center, axis=-1, keepdims=True)
    return center * lax.rsqrt(spread + 1e-05)


def tile_rows(positions, tile_table, length):
    tile_count = tile_table.shape[0]
    tile_width = length // tile_count
    onehot = (positions[:, None] // tile_width == jnp.arange(tile_count)[None, :]).astype(
        jnp.float32
    )
    picked = jnp.dot(onehot, tile_table.astype(jnp.float32))
    spread_out = jnp.broadcast_to(picked[:, :, None], (positions.shape[0], tile_count, tile_width))
    return spread_out.reshape(positions.shape[0], length) > 0.5


def tile_pairs(row_pos, col_pos, tile_table, length):
    tile_count = tile_table.shape[0]
    tile_width = length // tile_count
    row_hot = (row_pos[:, None] // tile_width == jnp.arange(tile_count)[None, :]).astype(
        jnp.float32
    )
    col_hot = (col_pos[:, None] // tile_width == jnp.arange(tile_count)[None, :]).astype(
        jnp.float32
    )
    return jnp.dot(jnp.dot(row_hot, tile_table.astype(jnp.float32)), col_hot.T)


def attend_lines(
    queries,
    key_rows,
    value_rows,
    gate_pre,
    bias_all,
    key_ok,
    chain_ids,
    chain_add,
    line_dim,
    flipped,
):
    length = queries.shape[1 - line_dim]
    head_count = queries.shape[2]
    head_size = queries.shape[3]
    width_all = head_count * head_size
    query_rows = min(128, length)
    blocks = length // query_rows
    scaling = head_size ** (-0.5)
    spec_q = "lqhd" if line_dim == 0 else "qlhd"
    spec_k = "lkhd" if line_dim == 0 else "klhd"
    usable = key_ok[:, None, None, :]
    if flipped:
        bias_all = bias_all.transpose(0, 2, 1)
    same_all = (chain_ids[:, None] == chain_ids[None, :]).astype(jnp.float32)
    bias_all = bias_all + chain_add[:, None, None] * same_all[None]

    def one_block(offset):
        query_block = lax.dynamic_slice_in_dim(queries, offset, query_rows, 1 - line_dim)
        scores = (
            jnp.einsum(
                f"{spec_q},{spec_k}->lhqk",
                query_block,
                key_rows,
                preferred_element_type=jnp.float32,
            )
            * scaling
        )
        bias_block = lax.dynamic_slice_in_dim(bias_all, offset, query_rows, 1)
        scores = scores + bias_block[None]
        scores = jnp.where(usable, scores, -1000000000.0)
        row_peak = jnp.max(scores, axis=-1, keepdims=True)
        weights = jnp.exp(scores - row_peak)
        attention = (weights / jnp.sum(weights, axis=-1, keepdims=True)).astype(jnp.bfloat16)
        mixed_rows = jnp.einsum(
            f"lhqk,{spec_k}->{spec_q}", attention, value_rows, preferred_element_type=jnp.float32
        )
        mixed_rows = mixed_rows.reshape(mixed_rows.shape[:2] + (width_all,))
        gate_block = lax.dynamic_slice_in_dim(gate_pre, offset, query_rows, 1 - line_dim)
        return (mixed_rows * jax.nn.sigmoid(gate_block)).astype(jnp.bfloat16)

    if blocks == 1:
        return one_block(0)
    outputs = lax.map(one_block, jnp.arange(blocks, dtype=jnp.int32) * query_rows)
    if line_dim == 0:
        outputs = outputs.transpose(1, 0, 2, 3)
    return outputs.reshape(gate_pre.shape[:2] + (width_all,))


def tri_acts(normed, weights, allowed):
    channels = normed.shape[-1]
    projected = jnp.dot(normed.reshape(-1, channels), weights, preferred_element_type=jnp.float32)
    projected = projected.reshape(normed.shape[0], normed.shape[1], 2 * channels)
    return (
        jax.nn.sigmoid(projected[..., channels:]) * projected[..., :channels] * allowed[..., None]
    ).astype(jnp.bfloat16)


def gather_lines(piece):
    device_count = lax.axis_size("row") * lax.axis_size("col")
    sent = jnp.broadcast_to(piece[None], (device_count,) + piece.shape)
    got = lax.all_to_all(sent, ("row", "col"), 0, 0, tiled=True)
    heads, rows_here, length = piece.shape
    return got.transpose(1, 0, 2, 3).reshape(heads, device_count * rows_here, length)


def shards(
    pair_rep,
    tile_mask,
    chain_ids,
    chain_bias,
    row_project,
    row_bias_proj,
    row_output,
    col_project,
    col_bias_proj,
    col_output,
    tri_left,
    tri_right,
    tri_gate,
    tri_output,
):
    n_row = lax.axis_size("row")
    n_col = lax.axis_size("col")
    device_count = n_row * n_col
    rows_here, length, channels = pair_rep.shape
    head_count = row_bias_proj.shape[1]
    head_size = channels // head_count
    row_index = lax.axis_index("row")
    col_index = lax.axis_index("col")
    device_index = row_index * n_col + col_index
    block_rows = length // n_row
    block_cols = length // n_col
    local_lines = device_index * rows_here + jnp.arange(rows_here, dtype=jnp.int32)
    local_cols = (
        col_index * block_cols + row_index * rows_here + jnp.arange(rows_here, dtype=jnp.int32)
    )
    normed = layer_norm(pair_rep).astype(jnp.bfloat16)
    flat_rows = normed.reshape(rows_here * length, channels)
    bias_rows = jnp.dot(flat_rows, row_bias_proj, preferred_element_type=jnp.float32)
    bias_rows = bias_rows.reshape(rows_here, length, head_count).transpose(2, 0, 1)
    bias_all = gather_lines(bias_rows)
    projected = jnp.dot(flat_rows, row_project, preferred_element_type=jnp.float32).reshape(
        rows_here, length, 4 * channels
    )
    qkv_rows = (
        projected[..., : 3 * channels]
        .astype(jnp.bfloat16)
        .reshape(rows_here, length, 3, head_count, head_size)
    )
    key_ok = tile_rows(local_lines, tile_mask, length)
    mixed_rows = attend_lines(
        qkv_rows[:, :, 0],
        qkv_rows[:, :, 1],
        qkv_rows[:, :, 2],
        projected[..., 3 * channels :],
        bias_all,
        key_ok,
        chain_ids,
        chain_bias[0],
        0,
        False,
    )
    update = jnp.dot(
        mixed_rows.reshape(-1, channels), row_output, preferred_element_type=jnp.float32
    ).reshape(rows_here, length, channels)
    first_pair = (pair_rep.astype(jnp.float32) + update).astype(jnp.bfloat16)
    normed_first = layer_norm(first_pair).astype(jnp.bfloat16)
    bias_next = jnp.dot(
        normed_first.reshape(-1, channels), col_bias_proj, preferred_element_type=jnp.float32
    )
    bias_next = bias_next.reshape(rows_here, length, head_count).transpose(2, 0, 1)
    lanes = 128
    pair_chunks = (
        first_pair.reshape(rows_here, n_col, n_row, rows_here, channels)
        .transpose(2, 1, 0, 3, 4)
        .reshape(device_count, rows_here * rows_here * channels // lanes, lanes)
    )
    bias_high = bias_next.astype(jnp.bfloat16)
    bias_low = (bias_next - bias_high.astype(jnp.float32)).astype(jnp.bfloat16)
    bias_words = jnp.stack([bias_high, bias_low], axis=0).reshape(1, -1, lanes)
    bias_chunks = jnp.broadcast_to(bias_words, (device_count,) + bias_words.shape[1:])
    merged = lax.all_to_all(
        jnp.concatenate([pair_chunks, bias_chunks], axis=1), ("row", "col"), 0, 0, tiled=True
    )
    pair_rows = pair_chunks.shape[1]
    columns = (
        merged[:, :pair_rows]
        .reshape(device_count, rows_here, rows_here, channels)
        .transpose(2, 0, 1, 3)
        .reshape(rows_here, length, channels)
    )
    bias_got = (
        merged[:, pair_rows:]
        .reshape(device_count, 2, head_count, rows_here, length)
        .astype(jnp.float32)
    )
    bias_cols = (
        (bias_got[:, 0] + bias_got[:, 1]).transpose(1, 0, 2, 3).reshape(head_count, length, length)
    )
    normed_cols = layer_norm(columns).astype(jnp.bfloat16)
    projected_cols = jnp.dot(
        normed_cols.reshape(-1, channels), col_project, preferred_element_type=jnp.float32
    ).reshape(rows_here, length, 4 * channels)
    qkv_cols = (
        projected_cols[..., : 3 * channels]
        .astype(jnp.bfloat16)
        .reshape(rows_here, length, 3, head_count, head_size)
    )
    col_ok = tile_rows(local_cols, tile_mask.T, length)
    mixed_cols = attend_lines(
        qkv_cols[:, :, 0],
        qkv_cols[:, :, 1],
        qkv_cols[:, :, 2],
        projected_cols[..., 3 * channels :],
        bias_cols,
        col_ok,
        chain_ids,
        chain_bias[1],
        0,
        True,
    )
    update_cols = jnp.dot(
        mixed_cols.reshape(-1, channels), col_output, preferred_element_type=jnp.float32
    ).reshape(rows_here, length, channels)
    second_pair = (columns.astype(jnp.float32) + update_cols).astype(jnp.bfloat16)
    normed_second = layer_norm(second_pair).astype(jnp.bfloat16)
    edge_mask = tile_pairs(local_cols, jnp.arange(length, dtype=jnp.int32), tile_mask.T, length)
    both = jnp.dot(
        normed_second.reshape(-1, channels),
        jnp.concatenate([tri_left, tri_right], axis=1),
        preferred_element_type=jnp.float32,
    ).reshape(normed_second.shape[:2] + (4 * channels,))
    left_all, right_all = (
        (jax.nn.sigmoid(half[..., channels:]) * half[..., :channels] * edge_mask[..., None]).astype(
            jnp.bfloat16
        )
        for half in (both[..., : 2 * channels], both[..., 2 * channels :])
    )
    channels_here = channels // device_count
    edges = jnp.stack([left_all, right_all], axis=0).transpose(3, 0, 1, 2)
    edges_got = lax.all_to_all(edges, ("row", "col"), 0, 2, tiled=True)
    product_part = jnp.einsum(
        "cki,ckj->cij", edges_got[:, 0], edges_got[:, 1], preferred_element_type=jnp.float32
    )
    product_sent = (
        product_part.reshape(channels_here, n_row, block_rows, n_col, block_cols)
        .transpose(1, 3, 0, 2, 4)
        .reshape(device_count, channels_here, block_rows, block_cols)
    )
    raw_chunks = second_pair.reshape(rows_here, n_row, block_rows, channels).transpose(1, 2, 0, 3)
    early = n_row // 2
    raw_pieces = [lax.dynamic_index_in_dim(raw_chunks, row_index, 0, keepdims=False)]
    for shift in range(1, n_row):
        if shift == early + 1:
            product_sent, raw_chunks = lax.optimization_barrier((product_sent, raw_chunks))
        piece = lax.dynamic_index_in_dim(raw_chunks, (row_index + shift) % n_row, 0, keepdims=False)
        raw_pieces.append(
            lax.ppermute(piece, "row", perm=[(r, (r + shift) % n_row) for r in range(n_row)])
        )
    sources = (row_index - jnp.arange(n_row, dtype=jnp.int32)) % n_row
    raw_got = jnp.take(jnp.stack(raw_pieces, axis=0), sources, axis=0)
    own_pair = raw_got.transpose(1, 0, 2, 3).reshape(block_rows, block_cols, channels)
    product_got = lax.all_to_all(
        product_sent.reshape(device_count, -1, lanes), ("row", "col"), 0, 0, tiled=True
    )
    product_sum = product_got.reshape(channels, block_rows, block_cols).transpose(1, 2, 0)
    normed_own = layer_norm(own_pair).astype(jnp.bfloat16)
    gate_values = jax.nn.sigmoid(
        jnp.dot(normed_own.reshape(-1, channels), tri_gate, preferred_element_type=jnp.float32)
    ).reshape(block_rows, block_cols, channels)
    centered = layer_norm(product_sum).astype(jnp.bfloat16)
    update_tri = jnp.dot(
        centered.reshape(-1, channels), tri_output, preferred_element_type=jnp.float32
    ).reshape(block_rows, block_cols, channels)
    return (own_pair.astype(jnp.float32) + gate_values * update_tri).astype(jnp.bfloat16)


def solution(mesh):
    return jax.shard_map(
        shards,
        mesh=mesh,
        in_specs=(
            P(("row", "col"), None, None),
            P(),
            P(),
            P(),
            P(),
            P(),
            P(),
            P(),
            P(),
            P(),
            P(),
            P(),
            P(),
            P(),
        ),
        out_specs=P("row", "col", None),
        check_vma=False,
    )
```

profile of v0, /device:TPU:0, one launch (start us, length us, event | category | flops | bytes accessed | tf_op | source)
XLA Modules:
  0.0 80.6 jit_solution(5535929860434226173)
XLA Ops:
  0.0 1.1 %convert_reduce_fusion = f32[4,128]{1,0:T(4,128)S(1)} fusion(bf16[4,128,128]{2,1,0:T(8,128)(2,1)} %param.14), kind=kLoop, calls=%fused_computation.39 | loop fusion | flops 130560 | bytes 133120 | tf_op jit(solution)/shard_map/reduce_sum | solution.py:9
  1.1 0.2 fusion.26
  1.4 0.7 copy-done.13
  2.0 0.3 convolution_bitcast_fusion.1
  2.4 0.7 broadcast_in_dim.33
  3.1 7.3 %all-to-all-start = ((f32[32,4,4,128]{3,2,1,0:T(4,128)}), f32[32,4,4,128]{3,2,1,0:T(4,128)S(1)}, u32[]{:S(2)}, u32[]{:S(2)}) async-start(f32[32,4,4,128]{3,2,1,0:T(4,128)} %broadcast_in_dim.33), calls=%async_computation | async-start | bytes 524288 | tf_op jit(solution)/shard_map/all_to_all | solution.py:108
  11.1 0.4 fusion.64
  11.5 0.2 copy.138
  11.8 0.6 copy-done.9
  12.4 0.6 copy-done.8
  13.2 7.5 %all-to-all-done = f32[32,4,4,128]{3,2,1,0:T(4,128)S(1)} async-done(((f32[32,4,4,128]{3,2,1,0:T(4,128)}), f32[32,4,4,128]{3,2,1,0:T(4,128)S(1)}, u32[]{:S(2)}, u32[]{:S(2)}) %all-to-all-start) | async-done | bytes 262176 | tf_op jit(solution)/shard_map/all_to_all | solution.py:108
  20.9 0.4 fusion.7
  21.3 0.6 fusion.102
  21.9 0.3 fusion.18
  22.4 0.6 copy-done.10
  23.0 0.3 convert_reduce_fusion.2
  23.3 0.2 fusion.30
  23.6 0.7 copy-done.14
  24.2 0.3 convert_bitcast_fusion.2
  24.7 0.8 pad_maximum_fusion
  25.4 2.7 %all-to-all-start.1 = ((bf16[32,48,128]{2,1,0:T(8,128)(2,1)}), bf16[32,48,128]{2,1,0:T(8,128)(2,1)S(1)}, u32[]{:S(2)}, u32[]{:S(2)}) async-start(bf16[32,48,128]{2,1,0:T(8,128)(2,1)} %pad_maximum_fusion), calls=%async_computation.1 | async-start | bytes 786432 | tf_op jit(solution)/shard_map/all_to_all | solution.py:189
  28.4 11.6 %all-to-all-done.1 = bf16[32,48,128]{2,1,0:T(8,128)(2,1)S(1)} async-done(((bf16[32,48,128]{2,1,0:T(8,128)(2,1)}), bf16[32,48,128]{2,1,0:T(8,128)(2,1)S(1)}, u32[]{:S(2)}, u32[]{:S(2)}) %all-to-all-start.1) | async-done | bytes 393248 | tf_op jit(solution)/shard_map/all_to_all | solution.py:189
  40.2 0.3 multiply_reduce_fusion.2
  40.8 0.2 copy.150
  41.1 0.6 copy-done.2
  41.7 0.3 fusion.54
  42.1 0.2 copy.153
  42.6 0.2 copy.158
  43.2 0.4 fusion.9
  43.5 0.6 fusion.103
  44.1 0.3 fusion.19
  44.6 0.8 %copy-done.3 = f32[4,32,4,128]{3,2,1,0:T(4,128)S(1)} copy-done((f32[4,32,4,128]{3,2,1,0:T(4,128)S(1)}, f32[4,32,4,128]{3,2,1,0:T(4,128)}, u32[]{:S(2)}) %copy-start.3) | copy-done | bytes 262168
  45.4 0.3 convert_reduce_fusion.1
  45.7 0.2 fusion.28
  46.0 0.6 copy-done.5
  46.6 0.4 fusion.58
  46.9 0.2 fusion.76
  47.2 0.9 %copy.168 = bf16[128,2,4,128]{3,2,1,0:T(4,128)(2,1)} copy(bf16[128,2,4,128]{0,3,2,1:T(8,128)(2,1)S(1)} %maximum_bitcast_fusion) | data formatting | bytes 524288 | tf_op jit(solution)/shard_map/transpose | solution.py:247
  48.0 3.8 %all-to-all-start.2 = ((bf16[128,2,4,128]{3,2,1,0:T(4,128)(2,1)}), bf16[128,2,4,128]{3,2,1,0:T(4,128)(2,1)S(1)}, u32[]{:S(2)}, u32[]{:S(2)}) async-start(bf16[128,2,4,128]{3,2,1,0:T(4,128)(2,1)} %copy.168), calls=%async_computation.2 | async-start | bytes 524288 | tf_op jit(solution)/shard_map/all_to_all | solution.py:248
  51.9 0.3 collective-permute-start
  52.2 1.6 %collective-permute-start.1 = (bf16[16,4,128]{2,0,1:T(8,128)(2,1)S(1)}, bf16[16,4,128]{2,0,1:T(8,128)(2,1)S(1)}, u32[]{:S(2)}, u32[]{:S(2)}) collective-permute-start(bf16[16,4,128]{2,0,1:T(8,128)(2,1)S(1)} %get-tuple-element.18), channel_id=1, source_target_pairs={{0,8},{4,12},{8,16},{12,20},{16,24},{20,28},{24,0},{28,4},{1,9},{5... | collective-permute-start | bytes 49160 | tf_op jit(solution)/shard_map/ppermute | solution.py:265
  53.8 2.3 %collective-permute-start.2 = (bf16[16,4,128]{2,0,1:T(8,128)(2,1)S(1)}, bf16[16,4,128]{2,0,1:T(8,128)(2,1)S(1)}, u32[]{:S(2)}, u32[]{:S(2)}) collective-permute-start(bf16[16,4,128]{2,0,1:T(8,128)(2,1)S(1)} %get-tuple-element.17), channel_id=1, source_target_pairs={{0,12},{4,16},{8,20},{12,24},{16,28},{20,0},{24,4},{28,8},{1,13},{... | collective-permute-start | bytes 49160 | tf_op jit(solution)/shard_map/ppermute | solution.py:265
  56.1 0.6 collective-permute-start.3
  56.6 0.3 collective-permute-done.1
  57.0 0.8 %collective-permute-done.2 = bf16[16,4,128]{2,0,1:T(8,128)(2,1)S(1)} collective-permute-done((bf16[16,4,128]{2,0,1:T(8,128)(2,1)S(1)}, bf16[16,4,128]{2,0,1:T(8,128)(2,1)S(1)}, u32[]{:S(2)}, u32[]{:S(2)}) %collective-permute-start.2) | collective-permute-done | bytes 16416 | tf_op jit(solution)/shard_map/ppermute | solution.py:265
  57.8 4.3 %all-to-all-done.2 = bf16[128,2,4,128]{3,2,1,0:T(4,128)(2,1)S(1)} async-done(((bf16[128,2,4,128]{3,2,1,0:T(4,128)(2,1)}), bf16[128,2,4,128]{3,2,1,0:T(4,128)(2,1)S(1)}, u32[]{:S(2)}, u32[]{:S(2)}) %all-to-all-start.2) | async-done | bytes 262176 | tf_op jit(solution)/shard_map/all_to_all | solution.py:248
  62.1 0.2 copy.170
  62.3 0.2 fusion.60
  62.6 0.4 reshape.439
  63.2 0.9 %collective-permute-start.4 = (bf16[16,4,128]{2,0,1:T(8,128)(2,1)S(1)}, bf16[16,4,128]{2,0,1:T(8,128)(2,1)S(1)}, u32[]{:S(2)}, u32[]{:S(2)}) collective-permute-start(bf16[16,4,128]{2,0,1:T(8,128)(2,1)S(1)} %get-tuple-element.15), channel_id=1, source_target_pairs={{0,20},{4,24},{8,28},{12,0},{16,4},{20,8},{24,12},{28,16},{1,21},{... | collective-permute-start | bytes 49160 | tf_op jit(solution)/shard_map/ppermute | solution.py:265
  64.1 1.0 %reshape.442 = f32[32,16,128]{2,1,0:T(8,128)} reshape(f32[32,4,16,32]{3,2,1,0:T(8,128)S(1)} %bitcast.218) | data formatting | bytes 524288 | tf_op jit(solution)/shard_map/reshape | solution.py:271
  65.1 3.0 %all-to-all-start.3 = ((f32[32,16,128]{2,1,0:T(8,128)}), f32[32,16,128]{2,1,0:T(8,128)S(1)}, u32[]{:S(2)}, u32[]{:S(2)}) async-start(f32[32,16,128]{2,1,0:T(8,128)} %reshape.442), calls=%async_computation.3 | async-start | bytes 524288 | tf_op jit(solution)/shard_map/all_to_all | solution.py:270
  68.1 2.7 %collective-permute-start.5 = (bf16[16,4,128]{2,0,1:T(8,128)(2,1)S(1)}, bf16[16,4,128]{2,0,1:T(8,128)(2,1)S(1)}, u32[]{:S(2)}, u32[]{:S(2)}) collective-permute-start(bf16[16,4,128]{2,0,1:T(8,128)(2,1)S(1)} %get-tuple-element.14), channel_id=1, source_target_pairs={{0,24},{4,28},{8,0},{12,4},{16,8},{20,12},{24,16},{28,20},{1,25},{... | collective-permute-start | bytes 49160 | tf_op jit(solution)/shard_map/ppermute | solution.py:265
  70.8 1.4 %collective-permute-done.5 = bf16[16,4,128]{2,0,1:T(8,128)(2,1)S(1)} collective-permute-done((bf16[16,4,128]{2,0,1:T(8,128)(2,1)S(1)}, bf16[16,4,128]{2,0,1:T(8,128)(2,1)S(1)}, u32[]{:S(2)}, u32[]{:S(2)}) %collective-permute-start.5) | collective-permute-done | bytes 16416 | tf_op jit(solution)/shard_map/ppermute | solution.py:265
  72.4 0.6 gather_fusion
  73.0 0.2 fusion.55
  73.2 0.3 multiply_reduce_fusion.1
  74.2 0.6 copy-done.12
  74.9 0.3 fusion.13
  75.2 3.1 %all-to-all-done.3 = f32[32,16,128]{2,1,0:T(8,128)S(1)} async-done(((f32[32,16,128]{2,1,0:T(8,128)}), f32[32,16,128]{2,1,0:T(8,128)S(1)}, u32[]{:S(2)}, u32[]{:S(2)}) %all-to-all-start.3) | async-done | bytes 262176 | tf_op jit(solution)/shard_map/all_to_all | solution.py:270
  78.3 0.3 reshape.443
  78.7 0.2 multiply_reduce_fusion
  79.1 0.6 copy-done.7
  79.7 1.0 %fusion.16 = bf16[16,32,128]{2,1,0:T(8,128)(2,1)} fusion(f32[16,32,128]{2,1,0:T(8,128)S(1)} %bitcast.231, f32[16,32,128]{2,1,0:T(8,128)S(1)} %bitcast.242, bf16[16,32,128]{1,0,2:T(8,128)(2,1)S(1)} %multiply_convert_fusion, bf16[128,128]{1,0:T(8,128)(2,1)S(1)} %copy-done.7), kind=kOutput, calls=%fused_computation.23 | convolution fusion | flops 16973824 | bytes 819200 | tf_op jit(solution)/shard_map/dot_general | solution.py:279
  (93 shorter events, 3.7 us)
Async XLA Ops:
  0.0 11.1 %copy-start = (bf16[128,512]{1,0:T(8,128)(2,1)S(1)}, bf16[128,512]{1,0:T(8,128)(2,1)}, u32[]{:S(2)}) copy-start(bf16[128,512]{1,0:T(8,128)(2,1)} %param.18) | copy-start | bytes 393220
  0.0 1.1 %copy-start.1 = (bf16[4,128,128]{2,1,0:T(8,128)(2,1)S(1)}, bf16[4,128,128]{2,1,0:T(8,128)(2,1)}, u32[]{:S(2)}) copy-start(bf16[4,128,128]{2,1,0:T(8,128)(2,1)} %param.14) | copy-start | bytes 393220
  1.4 0.7 copy-start.13
  3.1 17.6 %all-to-all-start = ((f32[32,4,4,128]{3,2,1,0:T(4,128)}), f32[32,4,4,128]{3,2,1,0:T(4,128)S(1)}, u32[]{:S(2)}, u32[]{:S(2)}) async-start(f32[32,4,4,128]{3,2,1,0:T(4,128)} %broadcast_in_dim.33), calls=%async_computation | async-start | bytes 524288 | tf_op jit(solution)/shard_map/all_to_all | solution.py:108
  11.8 0.7 copy-start.9
  12.4 0.7 copy-start.8
  22.2 0.8 copy-start.10
  23.5 0.7 copy-start.14
  25.4 14.5 %all-to-all-start.1 = ((bf16[32,48,128]{2,1,0:T(8,128)(2,1)}), bf16[32,48,128]{2,1,0:T(8,128)(2,1)S(1)}, u32[]{:S(2)}, u32[]{:S(2)}) async-start(bf16[32,48,128]{2,1,0:T(8,128)(2,1)} %pad_maximum_fusion), calls=%async_computation.1 | async-start | bytes 786432 | tf_op jit(solution)/shard_map/all_to_all | solution.py:189
  40.8 0.9 %copy-start.4 = (bf16[128,512]{1,0:T(8,128)(2,1)S(1)}, bf16[128,512]{1,0:T(8,128)(2,1)}, u32[]{:S(2)}) copy-start(bf16[128,512]{1,0:T(8,128)(2,1)} %param.21) | copy-start | bytes 393220
  41.0 0.7 copy-start.2
  44.4 1.0 %copy-start.3 = (f32[4,32,4,128]{3,2,1,0:T(4,128)S(1)}, f32[4,32,4,128]{3,2,1,0:T(4,128)}, u32[]{:S(2)}) copy-start(f32[4,32,4,128]{3,2,1,0:T(4,128)} %copy-done.2) | copy-start | bytes 786436
  44.4 1.0 %copy-start.11 = (bf16[128,128]{1,0:T(8,128)(2,1)S(1)}, bf16[128,128]{1,0:T(8,128)(2,1)}, u32[]{:S(2)}) copy-start(bf16[128,128]{1,0:T(8,128)(2,1)} %param.23) | copy-start | bytes 98308
  45.7 0.8 %copy-start.5 = (bf16[128,256]{1,0:T(8,128)(2,1)S(1)}, bf16[128,256]{1,0:T(8,128)(2,1)}, u32[]{:S(2)}) copy-start(bf16[128,256]{1,0:T(8,128)(2,1)} %param.25) | copy-start | bytes 196612
  45.7 0.9 %copy-start.6 = (bf16[128,256]{1,0:T(8,128)(2,1)S(1)}, bf16[128,256]{1,0:T(8,128)(2,1)}, u32[]{:S(2)}) copy-start(bf16[128,256]{1,0:T(8,128)(2,1)} %param.24) | copy-start | bytes 196612
  48.0 14.1 %all-to-all-start.2 = ((bf16[128,2,4,128]{3,2,1,0:T(4,128)(2,1)}), bf16[128,2,4,128]{3,2,1,0:T(4,128)(2,1)S(1)}, u32[]{:S(2)}, u32[]{:S(2)}) async-start(bf16[128,2,4,128]{3,2,1,0:T(4,128)(2,1)} %copy.168), calls=%async_computation.2 | async-start | bytes 524288 | tf_op jit(solution)/shard_map/all_to_all | solution.py:248
  51.9 4.8 %collective-permute-start = (bf16[16,4,128]{2,0,1:T(8,128)(2,1)S(1)}, bf16[16,4,128]{2,0,1:T(8,128)(2,1)S(1)}, u32[]{:S(2)}, u32[]{:S(2)}) collective-permute-start(bf16[16,4,128]{2,0,1:T(8,128)(2,1)S(1)} %get-tuple-element.19), channel_id=1, source_target_pairs={{0,4},{4,8},{8,12},{12,16},{16,20},{20,24},{24,28},{28,0},{1,5},{5... | collective-permute-start | bytes 49160 | tf_op jit(solution)/shard_map/ppermute | solution.py:265
  52.2 4.8 %collective-permute-start.1 = (bf16[16,4,128]{2,0,1:T(8,128)(2,1)S(1)}, bf16[16,4,128]{2,0,1:T(8,128)(2,1)S(1)}, u32[]{:S(2)}, u32[]{:S(2)}) collective-permute-start(bf16[16,4,128]{2,0,1:T(8,128)(2,1)S(1)} %get-tuple-element.18), channel_id=1, source_target_pairs={{0,8},{4,12},{8,16},{12,20},{16,24},{20,28},{24,0},{28,4},{1,9},{5... | collective-permute-start | bytes 49160 | tf_op jit(solution)/shard_map/ppermute | solution.py:265
  53.8 4.0 %collective-permute-start.2 = (bf16[16,4,128]{2,0,1:T(8,128)(2,1)S(1)}, bf16[16,4,128]{2,0,1:T(8,128)(2,1)S(1)}, u32[]{:S(2)}, u32[]{:S(2)}) collective-permute-start(bf16[16,4,128]{2,0,1:T(8,128)(2,1)S(1)} %get-tuple-element.17), channel_id=1, source_target_pairs={{0,12},{4,16},{8,20},{12,24},{16,28},{20,0},{24,4},{28,8},{1,13},{... | collective-permute-start | bytes 49160 | tf_op jit(solution)/shard_map/ppermute | solution.py:265
  56.1 8.0 %collective-permute-start.3 = (bf16[16,4,128]{2,0,1:T(8,128)(2,1)S(1)}, bf16[16,4,128]{2,0,1:T(8,128)(2,1)S(1)}, u32[]{:S(2)}, u32[]{:S(2)}) collective-permute-start(bf16[16,4,128]{2,0,1:T(8,128)(2,1)S(1)} %get-tuple-element.16), channel_id=1, source_target_pairs={{0,16},{4,20},{8,24},{12,28},{16,0},{20,4},{24,8},{28,12},{1,17},{... | collective-permute-start | bytes 49160 | tf_op jit(solution)/shard_map/ppermute | solution.py:265
  63.2 7.6 %collective-permute-start.4 = (bf16[16,4,128]{2,0,1:T(8,128)(2,1)S(1)}, bf16[16,4,128]{2,0,1:T(8,128)(2,1)S(1)}, u32[]{:S(2)}, u32[]{:S(2)}) collective-permute-start(bf16[16,4,128]{2,0,1:T(8,128)(2,1)S(1)} %get-tuple-element.15), channel_id=1, source_target_pairs={{0,20},{4,24},{8,28},{12,0},{16,4},{20,8},{24,12},{28,16},{1,21},{... | collective-permute-start | bytes 49160 | tf_op jit(solution)/shard_map/ppermute | solution.py:265
  65.1 13.2 %all-to-all-start.3 = ((f32[32,16,128]{2,1,0:T(8,128)}), f32[32,16,128]{2,1,0:T(8,128)S(1)}, u32[]{:S(2)}, u32[]{:S(2)}) async-start(f32[32,16,128]{2,1,0:T(8,128)} %reshape.442), calls=%async_computation.3 | async-start | bytes 524288 | tf_op jit(solution)/shard_map/all_to_all | solution.py:270
  68.1 4.2 %collective-permute-start.5 = (bf16[16,4,128]{2,0,1:T(8,128)(2,1)S(1)}, bf16[16,4,128]{2,0,1:T(8,128)(2,1)S(1)}, u32[]{:S(2)}, u32[]{:S(2)}) collective-permute-start(bf16[16,4,128]{2,0,1:T(8,128)(2,1)S(1)} %get-tuple-element.14), channel_id=1, source_target_pairs={{0,24},{4,28},{8,0},{12,4},{16,8},{20,12},{24,16},{28,20},{1,25},{... | collective-permute-start | bytes 49160 | tf_op jit(solution)/shard_map/ppermute | solution.py:265
  70.8 1.6 %collective-permute-start.6 = (bf16[16,4,128]{2,0,1:T(8,128)(2,1)S(1)}, bf16[16,4,128]{2,0,1:T(8,128)(2,1)S(1)}, u32[]{:S(2)}, u32[]{:S(2)}) collective-permute-start(bf16[16,4,128]{2,0,1:T(8,128)(2,1)S(1)} %get-tuple-element.13), channel_id=1, source_target_pairs={{0,28},{4,0},{8,4},{12,8},{16,12},{20,16},{24,20},{28,24},{1,29},{... | collective-permute-start | bytes 49160 | tf_op jit(solution)/shard_map/ppermute | solution.py:265
  74.1 0.8 copy-start.12
  78.9 0.8 copy-start.7
where the time goes:
time: 81.4 us; the launch traced here: 80.6 us
  waiting for transfers between devices  29.2 us (36%)
  starting transfers between devices  25.2 us (31%)
  local copies, waits for them, and re-layouts  13.8 us (17%)
  matrix products  6.34 us (8%)
  other arithmetic  4.88 us (6%)
  between operations  1.33 us (2%)
    all_to_all x1, waiting for transfers between devices, shards(): lax.all_to_all(jnp.concatenate([pair_chunks, bias_chunks], axis=1), ('row...  11.6 us
    ppermute x7, starting transfers between devices, shards(): lax.ppermute(piece, 'row', perm=[(r, (r + shift) % n_row) for r in range(...  8.38 us
    all_to_all x1, waiting for transfers between devices, gather_lines(): got = lax.all_to_all(sent, ('row', 'col'), 0, 0, tiled=True)  7.48 us
    all_to_all x1, starting transfers between devices, gather_lines(): got = lax.all_to_all(sent, ('row', 'col'), 0, 0, tiled=True)  7.33 us
    unnamed x38, local copies, waits for them, and re-layouts  6.73 us
    all_to_all x1, waiting for transfers between devices, shards(): edges_got = lax.all_to_all(edges, ('row', 'col'), 0, 2, tiled=True)  4.28 us
    all_to_all x1, starting transfers between devices, shards(): edges_got = lax.all_to_all(edges, ('row', 'col'), 0, 2, tiled=True)  3.82 us
    all_to_all x1, waiting for transfers between devices, shards(): lax.all_to_all(product_sent.reshape(device_count, -1, lanes), ('row', 'co...  3.08 us
  transfers between devices with their start and end apart: 11, of which 8 were waited for; matrix products, arithmetic and copies ran while one was open for 6% of the time, Pallas kernels for 0%

commit v1 on v0

--- a/solution.py
+++ b/solution.py
@@ -245,7 +245,10 @@
     )
     channels_here = channels // device_count
     edges = jnp.stack([left_all, right_all], axis=0).transpose(3, 0, 1, 2)
-    edges_got = lax.all_to_all(edges, ("row", "col"), 0, 2, tiled=True)
+    size = lax.axis_size(("row", "col"))
+    tiles = jnp.stack(jnp.split(edges, size, axis=0), axis=0)
+    tiles = lax.all_to_all(tiles, ("row", "col"), split_axis=0, concat_axis=0)
+    edges_got = jnp.concatenate(tiles, axis=2)
     product_part = jnp.einsum(
         "cki,ckj->cij", edges_got[:, 0], edges_got[:, 1], preferred_element_type=jnp.float32
     )

time: 81.4 us -> 112 us (1.38)
  local copies, waits for them, and re-layouts: 13.8 us -> 41.6 us
  matrix products: 6.34 us -> 8.19 us
  other arithmetic: 4.88 us -> 6.52 us
    unnamed x38 -> x63, local copies, waits for them, and re-layouts: 6.73 us -> 26.9 us
    another operation x0 -> x2, local copies, waits for them, and re-layouts: none -> 7.89 us  [shards(): tiles = jnp.stack(jnp.split(edges, size, axis=0), axis=0)]
  transfers between devices with their start and end apart: 11 -> 11, of which waited for: 8 -> 8; matrix products, arithmetic and copies ran while one was open for 6% -> 7% of each run, Pallas kernels for 0% -> 0%
where the time goes in v1:
time: 112 us
  local copies, waits for them, and re-layouts  41.6 us (37%)
  waiting for transfers between devices  28.5 us (25%)
  starting transfers between devices  25.3 us (23%)
  matrix products  8.19 us (7%)
  other arithmetic  6.52 us (6%)
  between operations  1.36 us (1%)
    unnamed x63, local copies, waits for them, and re-layouts  26.9 us
    all_to_all x1, waiting for transfers between devices, shards(): lax.all_to_all(jnp.concatenate([pair_chunks, bias_chunks], axis=1), ('row...  11.4 us
    ppermute x7, starting transfers between devices, shards(): lax.ppermute(piece, 'row', perm=[(r, (r + shift) % n_row) for r in range(...  8.38 us
    another operation x2, local copies, waits for them, and re-layouts, shards(): tiles = jnp.stack(jnp.split(edges, size, axis=0), axis=0)  7.89 us
    all_to_all x1, starting transfers between devices, gather_lines(): got = lax.all_to_all(sent, ('row', 'col'), 0, 0, tiled=True)  7.33 us
    all_to_all x1, waiting for transfers between devices, gather_lines(): got = lax.all_to_all(sent, ('row', 'col'), 0, 0, tiled=True)  6.4 us
    all_to_all x1, waiting for transfers between devices, shards(): tiles = lax.all_to_all(tiles, ('row', 'col'), split_axis=0, concat_axis=0)  4.28 us
    all_to_all x1, starting transfers between devices, shards(): tiles = lax.all_to_all(tiles, ('row', 'col'), split_axis=0, concat_axis=0)  3.81 us
  transfers between devices with their start and end apart: 11, of which 8 were waited for; matrix products, arithmetic and copies ran while one was open for 7% of the time, Pallas kernels for 0%

profile of v1, /device:TPU:0, one launch (start us, length us, event | category | flops | bytes accessed | tf_op | source)
XLA Modules:
  0.0 111.5 jit_solution(16221252825036204550)
XLA Ops:
  0.0 1.1 convert_reduce_fusion
  1.1 1.1 %fusion.26 = f32[4,128]{1,0:T(4,128)S(1)} fusion(bf16[4,128,128]{2,1,0:T(8,128)(2,1)} %param.14, f32[4,128]{1,0:T(4,128)S(1)} %broadcast_multiply_fusion.5), kind=kLoop, calls=%fused_computation.50 | loop fusion | flops 261632 | bytes 135168 | tf_op jit(solution)/shard_map/reduce_sum | solution.py:10
  2.3 1.2 %convolution_bitcast_fusion.1 = f32[4,4,128]{2,0,1:T(4,128)S(1)} fusion(bf16[4,128,128]{2,1,0:T(8,128)(2,1)} %param.14, f32[4,128]{1,0:T(4,128)S(1)} %add_rsqrt_fusion.4, f32[4,128]{1,0:T(4,128)S(1)} %broadcast_multiply_fusion.5, bf16[128,4]{0,1:T(4,128)(2,1)} %param.19), kind=kOutput, calls=%fused_computation.25 | convolution fusion | flops 786432 | bytes 144384 | tf_op jit(solution)/shard_map/dot_general | solution.py:146
  3.5 0.7 broadcast_in_dim.33
  4.2 7.3 %all-to-all-start = ((f32[32,4,4,128]{3,2,1,0:T(4,128)}), f32[32,4,4,128]{3,2,1,0:T(4,128)S(1)}, u32[]{:S(2)}, u32[]{:S(2)}) async-start(f32[32,4,4,128]{3,2,1,0:T(4,128)} %broadcast_in_dim.33), calls=%async_computation | async-start | bytes 524288 | tf_op jit(solution)/shard_map/all_to_all | solution.py:108
  12.2 1.3 %fusion.96 = f32[4,128,512]{2,1,0:T(8,128)S(1)} fusion(bf16[128,512]{1,0:T(8,128)(2,1)S(1)} %copy-done, bf16[4,128,128]{2,1,0:T(8,128)(2,1)} %param.14, f32[4,128]{1,0:T(4,128)S(1)} %add_rsqrt_fusion.4, f32[4,128]{1,0:T(4,128)S(1)} %broadcast_multiply_fusion.5), kind=kOutput, calls=%fused_computation.174 | convolution fusion | flops 67371008 | bytes 1314816 | tf_op jit(solution)/shard_map/dot_general | solution.py:149
  13.8 0.8 slice_bitcast_fusion.56
  14.6 0.8 compare_convert_fusion
  15.4 6.4 %all-to-all-done = f32[32,4,4,128]{3,2,1,0:T(4,128)S(1)} async-done(((f32[32,4,4,128]{3,2,1,0:T(4,128)}), f32[32,4,4,128]{3,2,1,0:T(4,128)S(1)}, u32[]{:S(2)}, u32[]{:S(2)}) %all-to-all-start) | async-done | bytes 262176 | tf_op jit(solution)/shard_map/all_to_all | solution.py:108
  22.1 0.4 fusion.7
  22.5 0.6 fusion.134
  24.6 0.8 pad_maximum_fusion
  25.3 2.8 %all-to-all-start.1 = ((bf16[32,48,128]{2,1,0:T(8,128)(2,1)}), bf16[32,48,128]{2,1,0:T(8,128)(2,1)S(1)}, u32[]{:S(2)}, u32[]{:S(2)}) async-start(bf16[32,48,128]{2,1,0:T(8,128)(2,1)} %pad_maximum_fusion), calls=%async_computation.1 | async-start | bytes 786432 | tf_op jit(solution)/shard_map/all_to_all | solution.py:189
  28.4 11.4 %all-to-all-done.1 = bf16[32,48,128]{2,1,0:T(8,128)(2,1)S(1)} async-done(((bf16[32,48,128]{2,1,0:T(8,128)(2,1)}), bf16[32,48,128]{2,1,0:T(8,128)(2,1)S(1)}, u32[]{:S(2)}, u32[]{:S(2)}) %all-to-all-start.1) | async-done | bytes 393248 | tf_op jit(solution)/shard_map/all_to_all | solution.py:189
  41.0 0.6 copy-done.2
  43.4 0.6 fusion.135
  45.6 0.7 fusion.63
  46.3 0.8 fusion.62
  47.2 0.8 fusion.61
  48.0 0.9 fusion.60
  48.9 0.9 fusion.59
  49.7 0.9 fusion.58
  50.6 0.8 fusion.57
  51.4 0.9 fusion.56
  52.3 0.9 fusion.55
  53.1 0.8 fusion.54
  54.0 0.8 fusion.53
  54.8 0.9 fusion.52
  55.7 0.9 fusion.51
  56.5 0.8 fusion.50
  57.4 0.8 fusion.49
  58.2 0.8 fusion.48
  59.1 0.8 fusion.47
  59.9 0.8 fusion.46
  60.8 0.8 fusion.45
  61.6 0.9 fusion.44
  62.5 0.8 fusion.43
  63.3 0.9 fusion.42
  64.2 0.8 fusion.41
  65.0 0.8 fusion.40
  65.9 0.8 fusion.39
  66.7 0.8 fusion.38
  67.6 0.9 fusion.37
  68.4 0.9 fusion.36
  69.3 0.8 fusion.35
  70.1 0.8 fusion.34
  70.9 0.8 fusion.33
  71.8 0.9 fusion.32
  72.6 7.0 %copy.239 = bf16[32,4,2,4,128]{4,3,2,1,0:T(4,128)(2,1)} copy(bf16[32,4,2,4,128]{1,4,3,2,0:T(8,128)(2,1)} %fusion.32) | data formatting | bytes 524288 | tf_op jit(solution)/shard_map/stack | solution.py:249
  79.7 3.8 %all-to-all-start.2 = ((bf16[32,4,2,4,128]{4,3,2,1,0:T(4,128)(2,1)}), bf16[32,4,2,4,128]{4,3,2,1,0:T(4,128)(2,1)S(1)}, u32[]{:S(2)}, u32[]{:S(2)}) async-start(bf16[32,4,2,4,128]{4,3,2,1,0:T(4,128)(2,1)} %copy.239), calls=%async_computation.2 | async-start | bytes 524288 | tf_op jit(solution)/shard_map/all_to_all | solution.py:250
  83.8 1.6 %collective-permute-start.1 = (bf16[16,4,128]{2,0,1:T(8,128)(2,1)S(1)}, bf16[16,4,128]{2,0,1:T(8,128)(2,1)S(1)}, u32[]{:S(2)}, u32[]{:S(2)}) collective-permute-start(bf16[16,4,128]{2,0,1:T(8,128)(2,1)S(1)} %get-tuple-element.18), channel_id=1, source_target_pairs={{0,8},{4,12},{8,16},{12,20},{16,24},{20,28},{24,0},{28,4},{1,9},{5... | collective-permute-start | bytes 49160 | tf_op jit(solution)/shard_map/ppermute | solution.py:268
  85.5 2.3 %collective-permute-start.2 = (bf16[16,4,128]{2,0,1:T(8,128)(2,1)S(1)}, bf16[16,4,128]{2,0,1:T(8,128)(2,1)S(1)}, u32[]{:S(2)}, u32[]{:S(2)}) collective-permute-start(bf16[16,4,128]{2,0,1:T(8,128)(2,1)S(1)} %get-tuple-element.17), channel_id=1, source_target_pairs={{0,12},{4,16},{8,20},{12,24},{16,28},{20,0},{24,4},{28,8},{1,13},{... | collective-permute-start | bytes 49160 | tf_op jit(solution)/shard_map/ppermute | solution.py:268
  87.7 0.6 collective-permute-start.3
  88.6 0.8 collective-permute-done.2
  89.4 4.3 %all-to-all-done.2 = bf16[32,4,2,4,128]{4,3,2,1,0:T(4,128)(2,1)S(1)} async-done(((bf16[32,4,2,4,128]{4,3,2,1,0:T(4,128)(2,1)}), bf16[32,4,2,4,128]{4,3,2,1,0:T(4,128)(2,1)S(1)}, u32[]{:S(2)}, u32[]{:S(2)}) %all-to-all-start.2) | async-done | bytes 262176 | tf_op jit(solution)/shard_map/all_to_all | solution.py:250
  94.1 0.4 reshape.447
  94.7 0.9 collective-permute-start.4
  95.6 1.0 reshape.450
  96.6 3.0 %all-to-all-start.3 = ((f32[32,16,128]{2,1,0:T(8,128)}), f32[32,16,128]{2,1,0:T(8,128)S(1)}, u32[]{:S(2)}, u32[]{:S(2)}) async-start(f32[32,16,128]{2,1,0:T(8,128)} %reshape.450), calls=%async_computation.3 | async-start | bytes 524288 | tf_op jit(solution)/shard_map/all_to_all | solution.py:273
  99.5 2.7 %collective-permute-start.5 = (bf16[16,4,128]{2,0,1:T(8,128)(2,1)S(1)}, bf16[16,4,128]{2,0,1:T(8,128)(2,1)S(1)}, u32[]{:S(2)}, u32[]{:S(2)}) collective-permute-start(bf16[16,4,128]{2,0,1:T(8,128)(2,1)S(1)} %get-tuple-element.14), channel_id=1, source_target_pairs={{0,24},{4,28},{8,0},{12,4},{16,8},{20,12},{24,16},{28,20},{1,25},{... | collective-permute-start | bytes 49160 | tf_op jit(solution)/shard_map/ppermute | solution.py:268
  102.3 1.4 %collective-permute-done.5 = bf16[16,4,128]{2,0,1:T(8,128)(2,1)S(1)} collective-permute-done((bf16[16,4,128]{2,0,1:T(8,128)(2,1)S(1)}, bf16[16,4,128]{2,0,1:T(8,128)(2,1)S(1)}, u32[]{:S(2)}, u32[]{:S(2)}) %collective-permute-start.5) | collective-permute-done | bytes 16416 | tf_op jit(solution)/shard_map/ppermute | solution.py:268
  103.9 0.6 gather_fusion
  106.1 3.7 %all-to-all-done.3 = f32[32,16,128]{2,1,0:T(8,128)S(1)} async-done(((f32[32,16,128]{2,1,0:T(8,128)}), f32[32,16,128]{2,1,0:T(8,128)S(1)}, u32[]{:S(2)}, u32[]{:S(2)}) %all-to-all-start.3) | async-done | bytes 262176 | tf_op jit(solution)/shard_map/all_to_all | solution.py:273
  110.5 1.0 fusion.16
  (118 shorter events, 10.2 us)
Async XLA Ops:
  0.0 12.2 %copy-start = (bf16[128,512]{1,0:T(8,128)(2,1)S(1)}, bf16[128,512]{1,0:T(8,128)(2,1)}, u32[]{:S(2)}) copy-start(bf16[128,512]{1,0:T(8,128)(2,1)} %param.18) | copy-start | bytes 393220
  0.0 23.5 %copy-start.1 = (bf16[4,128,128]{2,1,0:T(8,128)(2,1)S(1)}, bf16[4,128,128]{2,1,0:T(8,128)(2,1)}, u32[]{:S(2)}) copy-start(bf16[4,128,128]{2,1,0:T(8,128)(2,1)} %param.14) | copy-start | bytes 393220
  0.0 23.5 %copy-start.8 = (bf16[128,128]{1,0:T(8,128)(2,1)S(1)}, bf16[128,128]{1,0:T(8,128)(2,1)}, u32[]{:S(2)}) copy-start(bf16[128,128]{1,0:T(8,128)(2,1)} %param.20) | copy-start | bytes 98308
  0.0 24.1 %copy-start.11 = (bf16[128,4]{0,1:T(4,128)(2,1)S(1)}, bf16[128,4]{0,1:T(4,128)(2,1)}, u32[]{:S(2)}) copy-start(bf16[128,4]{0,1:T(4,128)(2,1)} %param.22) | copy-start | bytes 3076
  4.2 17.6 %all-to-all-start = ((f32[32,4,4,128]{3,2,1,0:T(4,128)}), f32[32,4,4,128]{3,2,1,0:T(4,128)S(1)}, u32[]{:S(2)}, u32[]{:S(2)}) async-start(f32[32,4,4,128]{3,2,1,0:T(4,128)} %broadcast_in_dim.33), calls=%async_computation | async-start | bytes 524288 | tf_op jit(solution)/shard_map/all_to_all | solution.py:108
  14.6 27.0 %copy-start.4 = (bf16[128,512]{1,0:T(8,128)(2,1)S(1)}, bf16[128,512]{1,0:T(8,128)(2,1)}, u32[]{:S(2)}) copy-start(bf16[128,512]{1,0:T(8,128)(2,1)} %param.21) | copy-start | bytes 393220
  25.3 14.5 %all-to-all-start.1 = ((bf16[32,48,128]{2,1,0:T(8,128)(2,1)}), bf16[32,48,128]{2,1,0:T(8,128)(2,1)S(1)}, u32[]{:S(2)}, u32[]{:S(2)}) async-start(bf16[32,48,128]{2,1,0:T(8,128)(2,1)} %pad_maximum_fusion), calls=%async_computation.1 | async-start | bytes 786432 | tf_op jit(solution)/shard_map/all_to_all | solution.py:189
  40.9 0.7 copy-start.2
  41.0 3.5 %copy-start.9 = (bf16[128,128]{1,0:T(8,128)(2,1)S(1)}, bf16[128,128]{1,0:T(8,128)(2,1)}, u32[]{:S(2)}) copy-start(bf16[128,128]{1,0:T(8,128)(2,1)} %param.23) | copy-start | bytes 98308
  41.9 3.1 %copy-start.5 = (bf16[128,256]{1,0:T(8,128)(2,1)S(1)}, bf16[128,256]{1,0:T(8,128)(2,1)}, u32[]{:S(2)}) copy-start(bf16[128,256]{1,0:T(8,128)(2,1)} %param.25) | copy-start | bytes 196612
  41.9 3.1 %copy-start.6 = (bf16[128,256]{1,0:T(8,128)(2,1)S(1)}, bf16[128,256]{1,0:T(8,128)(2,1)}, u32[]{:S(2)}) copy-start(bf16[128,256]{1,0:T(8,128)(2,1)} %param.24) | copy-start | bytes 196612
  42.4 2.1 %copy-start.3 = (f32[4,32,4,128]{3,2,1,0:T(4,128)S(1)}, f32[4,32,4,128]{3,2,1,0:T(4,128)}, u32[]{:S(2)}) copy-start(f32[4,32,4,128]{3,2,1,0:T(4,128)} %copy-done.2) | copy-start | bytes 786436
  72.6 33.1 %copy-start.10 = (bf16[128,128]{1,0:T(8,128)(2,1)S(1)}, bf16[128,128]{1,0:T(8,128)(2,1)}, u32[]{:S(2)}) copy-start(bf16[128,128]{1,0:T(8,128)(2,1)} %param.26) | copy-start | bytes 98308
  79.7 30.9 %copy-start.7 = (bf16[128,128]{1,0:T(8,128)(2,1)S(1)}, bf16[128,128]{1,0:T(8,128)(2,1)}, u32[]{:S(2)}) copy-start(bf16[128,128]{1,0:T(8,128)(2,1)} %param.27) | copy-start | bytes 98308
  79.7 14.0 %all-to-all-start.2 = ((bf16[32,4,2,4,128]{4,3,2,1,0:T(4,128)(2,1)}), bf16[32,4,2,4,128]{4,3,2,1,0:T(4,128)(2,1)S(1)}, u32[]{:S(2)}, u32[]{:S(2)}) async-start(bf16[32,4,2,4,128]{4,3,2,1,0:T(4,128)(2,1)} %copy.239), calls=%async_computation.2 | async-start | bytes 524288 | tf_op jit(solution)/shard_map/all_to_all | solution.py:250
  83.5 4.8 %collective-permute-start = (bf16[16,4,128]{2,0,1:T(8,128)(2,1)S(1)}, bf16[16,4,128]{2,0,1:T(8,128)(2,1)S(1)}, u32[]{:S(2)}, u32[]{:S(2)}) collective-permute-start(bf16[16,4,128]{2,0,1:T(8,128)(2,1)S(1)} %get-tuple-element.19), channel_id=1, source_target_pairs={{0,4},{4,8},{8,12},{12,16},{16,20},{20,24},{24,28},{28,0},{1,5},{5... | collective-permute-start | bytes 49160 | tf_op jit(solution)/shard_map/ppermute | solution.py:268
  83.8 4.8 %collective-permute-start.1 = (bf16[16,4,128]{2,0,1:T(8,128)(2,1)S(1)}, bf16[16,4,128]{2,0,1:T(8,128)(2,1)S(1)}, u32[]{:S(2)}, u32[]{:S(2)}) collective-permute-start(bf16[16,4,128]{2,0,1:T(8,128)(2,1)S(1)} %get-tuple-element.18), channel_id=1, source_target_pairs={{0,8},{4,12},{8,16},{12,20},{16,24},{20,28},{24,0},{28,4},{1,9},{5... | collective-permute-start | bytes 49160 | tf_op jit(solution)/shard_map/ppermute | solution.py:268
  85.5 4.0 %collective-permute-start.2 = (bf16[16,4,128]{2,0,1:T(8,128)(2,1)S(1)}, bf16[16,4,128]{2,0,1:T(8,128)(2,1)S(1)}, u32[]{:S(2)}, u32[]{:S(2)}) collective-permute-start(bf16[16,4,128]{2,0,1:T(8,128)(2,1)S(1)} %get-tuple-element.17), channel_id=1, source_target_pairs={{0,12},{4,16},{8,20},{12,24},{16,28},{20,0},{24,4},{28,8},{1,13},{... | collective-permute-start | bytes 49160 | tf_op jit(solution)/shard_map/ppermute | solution.py:268
  87.7 7.9 %collective-permute-start.3 = (bf16[16,4,128]{2,0,1:T(8,128)(2,1)S(1)}, bf16[16,4,128]{2,0,1:T(8,128)(2,1)S(1)}, u32[]{:S(2)}, u32[]{:S(2)}) collective-permute-start(bf16[16,4,128]{2,0,1:T(8,128)(2,1)S(1)} %get-tuple-element.16), channel_id=1, source_target_pairs={{0,16},{4,20},{8,24},{12,28},{16,0},{20,4},{24,8},{28,12},{1,17},{... | collective-permute-start | bytes 49160 | tf_op jit(solution)/shard_map/ppermute | solution.py:268
  94.7 7.6 %collective-permute-start.4 = (bf16[16,4,128]{2,0,1:T(8,128)(2,1)S(1)}, bf16[16,4,128]{2,0,1:T(8,128)(2,1)S(1)}, u32[]{:S(2)}, u32[]{:S(2)}) collective-permute-start(bf16[16,4,128]{2,0,1:T(8,128)(2,1)S(1)} %get-tuple-element.15), channel_id=1, source_target_pairs={{0,20},{4,24},{8,28},{12,0},{16,4},{20,8},{24,12},{28,16},{1,21},{... | collective-permute-start | bytes 49160 | tf_op jit(solution)/shard_map/ppermute | solution.py:268
  96.6 13.2 %all-to-all-start.3 = ((f32[32,16,128]{2,1,0:T(8,128)}), f32[32,16,128]{2,1,0:T(8,128)S(1)}, u32[]{:S(2)}, u32[]{:S(2)}) async-start(f32[32,16,128]{2,1,0:T(8,128)} %reshape.450), calls=%async_computation.3 | async-start | bytes 524288 | tf_op jit(solution)/shard_map/all_to_all | solution.py:273
  99.5 4.2 %collective-permute-start.5 = (bf16[16,4,128]{2,0,1:T(8,128)(2,1)S(1)}, bf16[16,4,128]{2,0,1:T(8,128)(2,1)S(1)}, u32[]{:S(2)}, u32[]{:S(2)}) collective-permute-start(bf16[16,4,128]{2,0,1:T(8,128)(2,1)S(1)} %get-tuple-element.14), channel_id=1, source_target_pairs={{0,24},{4,28},{8,0},{12,4},{16,8},{20,12},{24,16},{28,20},{1,25},{... | collective-permute-start | bytes 49160 | tf_op jit(solution)/shard_map/ppermute | solution.py:268
  102.3 1.6 %collective-permute-start.6 = (bf16[16,4,128]{2,0,1:T(8,128)(2,1)S(1)}, bf16[16,4,128]{2,0,1:T(8,128)(2,1)S(1)}, u32[]{:S(2)}, u32[]{:S(2)}) collective-permute-start(bf16[16,4,128]{2,0,1:T(8,128)(2,1)S(1)} %get-tuple-element.13), channel_id=1, source_target_pairs={{0,28},{4,0},{8,4},{12,8},{16,12},{20,16},{24,20},{28,24},{1,29},{... | collective-permute-start | bytes 49160 | tf_op jit(solution)/shard_map/ppermute | solution.py:268
